TPU v7x, 32 devices: a whole 2x2x4 slice. The times are simulated.
32 devices in a mesh: freq: 4 (over x, core), tm: 8 (over z, y).
Axes of the slice: x: 2, y: 2, z: 4, core: 2. Of those that a mesh axis runs over, the one named last changes fastest.
Arguments:
- signal: float32 [8388608], P('tm'), may hold values from -60 to 60, as said below
- w_init: float32 [2048, 256], P('freq'), may hold values from 0.02 to 0.2
- h_init: float32 [256, 8192], P(None, 'tm'), may hold values from 0.02 to 0.2
Outputs:
- factor_w: float32 [2048, 256], P('freq')
- factor_h: float32 [256, 8192], P(None, 'tm')
Inputs may be any that keep to these rules, and one draw needn't show every extreme that they name: `signal`: a broadband record with a few tones.
All inputs are finite; a program needn't handle non-finite values.
Results may differ from a plain program's by a relative error of at most 0.0004.
Values sent between devices are 32-bit elements; how exact they have to be, the bound alone decides.
No kernel may reach another device: no remote copies, remote signals or barrier semaphores. Data moves between devices by JAX's collectives and lax.ppermute only.
A program may use at most 128 MiB of HBM per device.

v0:
```python
import math

import jax
import jax.numpy as jnp
from jax import lax
from jax.sharding import PartitionSpec as P

WIN = 4096
HOP = 1024
K = 2048
ITERS = 2


def shifted(value, axis, by):
    size = lax.axis_size(axis)
    pairs = [(i, i + by) for i in range(size) if 0 <= i + by < size]
    return lax.ppermute(value, axis, pairs)


def dft_table(first, count):
    samples = jnp.arange(WIN, dtype=jnp.int32)
    bins = first + jnp.arange(count, dtype=jnp.int32)
    phase = samples[:, None] * bins[None, :] % WIN
    angle = phase.astype(jnp.float32) * (2.0 * math.pi / WIN)
    return jnp.concatenate([jnp.cos(angle), jnp.sin(angle)], axis=1).astype(jnp.bfloat16)


def hann_window():
    samples = jnp.arange(WIN, dtype=jnp.int32).astype(jnp.float32)
    return 0.5 - 0.5 * jnp.cos(samples * (2.0 * math.pi / WIN))


def cut_frames(blocks, count):
    steps_per = WIN // HOP
    frames = jnp.concatenate([blocks[j : j + count] for j in range(steps_per)], axis=1)
    return (frames * hann_window()[None, :]).astype(jnp.bfloat16)


def spectrum(windowed, table, count):
    both = jnp.einsum("wc,fw->cf", table, windowed, preferred_element_type=jnp.float32)
    real_part = both[:count]
    imag_part = both[count:]
    return (real_part * real_part + imag_part * imag_part) / (0.375 * WIN)


def local(signal, w_init, h_init):
    steps_per = WIN // HOP
    frames_dev = signal.shape[0] // HOP
    tail = shifted(signal[: (steps_per - 1) * HOP], "tm", -1)
    blocks = jnp.concatenate([signal, tail]).reshape(frames_dev + steps_per - 1, HOP)
    local_bins = K // lax.axis_size("freq")
    windowed = cut_frames(blocks, frames_dev)
    power = spectrum(
        windowed, dft_table(lax.axis_index("freq") * local_bins, local_bins), local_bins
    )
    factor_w = w_init
    factor_h = h_init
    for step in range(ITERS):
        model = jnp.dot(
            factor_w, factor_h, precision=lax.Precision.HIGHEST, preferred_element_type=jnp.float32
        )
        ratio = power / model
        numer = jnp.einsum("kr,kf->rf", factor_w, ratio, precision=lax.Precision.HIGHEST)
        column_sums = jnp.sum(factor_w, axis=0)
        numer, column_sums = lax.psum((numer, column_sums), "freq")
        factor_h = factor_h * numer / column_sums[:, None]
        model = jnp.dot(
            factor_w, factor_h, precision=lax.Precision.HIGHEST, preferred_element_type=jnp.float32
        )
        ratio = power / model
        row_sums = jnp.sum(factor_h, axis=1)
        spectral = jnp.einsum("kf,rf->kr", ratio, factor_h, precision=lax.Precision.HIGHEST)
        spectral, row_sums = lax.psum((spectral, row_sums), "tm")
        factor_w = factor_w * spectral / row_sums[None, :]
    return (factor_w, factor_h)


def solution(mesh):
    in_specs = (P("tm"), P("freq", None), P(None, "tm"))
    out_specs = (P("freq", None), P(None, "tm"))
    return jax.shard_map(local, mesh=mesh, in_specs=in_specs, out_specs=out_specs, check_vma=False)
```

profile of v0, /device:TPU:0, one launch (start us, length us, event | category | flops | bytes accessed | tf_op | source)
XLA Modules:
  0.0 361.2 jit_solution(10525891649220605073)
XLA Ops:
  7.9 1.3 collective-permute-start
  9.2 4.4 %constant_dynamic-update-slice_fusion.1 = f32[1051648]{0:T(1024)} fusion(f32[1048576]{0:T(1024)} %param.3), kind=kLoop, calls=%fused_computation.36 | loop fusion | bytes 8388608
  13.6 34.8 %cosine_convert_fusion = (bf16[4096,512]{1,0:T(8,128)(2,1)}, bf16[4096,512]{1,0:T(8,128)(2,1)}) fusion(s32[512]{0:T(512)S(1)} %iota_add_fusion), kind=kLoop, calls=%fused_computation.13 | loop fusion | flops 33554432 | bytes 8390656 | tf_op jit(solution)/shard_map/convert
  48.4 3.2 fusion.30
  51.7 4.9 %slice.57 = f32[1024,1024]{1,0:T(8,128)} reshape(f32[1048576]{0:T(1024)} %param.3) | data formatting | bytes 8388608 | tf_op jit(solution)/shard_map/slice | solution.py:35
  57.2 9.4 %fusion.29 = (f32[1048576]{0:T(1024)}, f32[1048576]{0:T(1024)}, f32[1048576]{0:T(1024)}) fusion(f32[1051648]{0:T(1024)} %constant_dynamic-update-slice_fusion), kind=kLoop, calls=%fused_computation.43 | loop fusion | bytes 25165824 | tf_op jit(solution)/shard_map/slice | solution.py:35
  66.6 4.9 %slice.60 = f32[1024,1024]{1,0:T(8,128)} reshape(f32[1048576]{0:T(1024)} %get-tuple-element.10) | data formatting | bytes 8388608 | tf_op jit(solution)/shard_map/slice | solution.py:35
  71.5 4.9 %slice.62 = f32[1024,1024]{1,0:T(8,128)} reshape(f32[1048576]{0:T(1024)} %get-tuple-element.12) | data formatting | bytes 8388608 | tf_op jit(solution)/shard_map/slice | solution.py:35
  76.4 4.9 %slice.64 = f32[1024,1024]{1,0:T(8,128)} reshape(f32[1048576]{0:T(1024)} %get-tuple-element.11) | data formatting | bytes 8388608 | tf_op jit(solution)/shard_map/slice | solution.py:35
  81.3 20.1 %fusion.4 = f32[1024,1024]{1,0:T(8,128)} fusion(bf16[4096,512]{1,0:T(8,128)(2,1)} %get-tuple-element.14, bf16[4096,512]{1,0:T(8,128)(2,1)} %get-tuple-element.13, f32[1024,1024]{1,0:T(8,128)} %slice.64, f32[1024,1024]{1,0:T(8,128)} %slice.62, f32[1024,1024]{1,0:T(8,128)} %slice.60, f32[1024,1024]{1,0:T(8,128)} %slice.57, f32[4096]{0:T(1024)S(1)} %multiply_subtract_fusion), kind=kOutput, calls=%fused_computation.8 | convolution fusion | flops 8627683328 | bytes 29376512 | tf_op jit(solution)/shard_map/wc,fw->cf/dot_general | solution.py:40
  101.3 2.8 fusion.13
  104.1 1.3 copy-done.2
  105.5 4.4 %fusion.21 = f32[256,1024]{0,1:T(8,128)} fusion(f32[512,256]{1,0:T(8,128)S(1)} %copy-done, f32[512,1024]{1,0:T(8,128)S(1)} %fusion.13, f32[512,1024]{1,0:T(8,128)S(1)} %copy-done.6), kind=kOutput, calls=%fused_computation.29 | convolution fusion | flops 1611137024 | bytes 5767168 | tf_op jit(solution)/shard_map/kr,kf->rf/dot_general | solution.py:63
  110.4 8.4 %psum.57 = f32[256]{0:T(256)S(1)} all-reduce(f32[256]{0:T(256)S(1)} %reduce_sum.36), channel_id=1, replica_groups=mesh['freq'=4,'tm'=8] {'freq'}, use_global_device_ids=true, to_apply=%region_2.3 | all-reduce | flops 256 | bytes 2048 | tf_op jit(solution)/shard_map/psum | solution.py:65
  118.8 31.4 %all-reduce.5.cloned.1.call-done = f32[256,1024]{0,1:T(8,128)} async-done(((f32[256,1024]{0,1:T(8,128)}), f32[256,1024]{0,1:T(8,128)}) %all-reduce.5.cloned.1.call-update) | async-done | bytes 1048592 | tf_op jit(solution)/shard_map/psum | solution.py:65
  150.3 1.6 fusion.28
  151.8 1.9 fusion.31
  153.7 2.7 fusion.14
  156.5 21.4 %psum.59 = f32[256]{0:T(256)S(1)} all-reduce(f32[256]{0:T(256)S(1)} %get-tuple-element.8), channel_id=1, replica_groups=mesh['freq'=4,'tm'=8] {'tm'}, use_global_device_ids=true, to_apply=%region_5.6 | all-reduce | flops 256 | bytes 2048 | tf_op jit(solution)/shard_map/psum | solution.py:73
  177.9 52.0 %all-reduce.7.cloned.1.call-done = f32[512,256]{1,0:T(8,128)} async-done(((f32[512,256]{1,0:T(8,128)}), f32[512,256]{1,0:T(8,128)}) %all-reduce.7.cloned.1.call-update) | async-done | bytes 524304 | tf_op jit(solution)/shard_map/psum | solution.py:73
  229.9 1.3 fusion.27
  231.2 1.9 fusion.32
  233.1 4.4 %fusion.17 = f32[256,1024]{0,1:T(8,128)} fusion(f32[512,256]{1,0:T(8,128)S(1)} %get-tuple-element.7, f32[512,1024]{1,0:T(8,128)S(1)} %copy-done.4, f32[512,1024]{1,0:T(8,128)S(1)} %fusion.32), kind=kOutput, calls=%fused_computation.25 | convolution fusion | flops 1611137024 | bytes 5767168 | tf_op jit(solution)/shard_map/kr,kf->rf/dot_general | solution.py:63
  237.6 5.7 %psum.61 = f32[256]{0:T(256)S(1)} all-reduce(f32[256]{0:T(256)S(1)} %get-tuple-element.6), channel_id=1, replica_groups=mesh['freq'=4,'tm'=8] {'freq'}, use_global_device_ids=true, to_apply=%region_8.9 | all-reduce | flops 256 | bytes 2048 | tf_op jit(solution)/shard_map/psum | solution.py:65
  243.3 29.9 %all-reduce.9.cloned.1.call-done = f32[256,1024]{0,1:T(8,128)} async-done(((f32[256,1024]{0,1:T(8,128)}), f32[256,1024]{0,1:T(8,128)}) %all-reduce.9.cloned.1.call-update) | async-done | bytes 1048592 | tf_op jit(solution)/shard_map/psum | solution.py:65
  273.2 1.6 fusion.26
  274.8 1.9 fusion.33
  276.7 2.7 fusion.15
  279.4 1.3 copy.7
  280.7 21.5 %psum.63 = f32[256]{0:T(256)S(1)} all-reduce(f32[256]{0:T(256)S(1)} %get-tuple-element.4), channel_id=1, replica_groups=mesh['freq'=4,'tm'=8] {'tm'}, use_global_device_ids=true, to_apply=%region_11.12 | all-reduce | flops 256 | bytes 2048 | tf_op jit(solution)/shard_map/psum | solution.py:73
  302.2 50.6 %all-reduce.11.cloned.1.call-done = f32[512,256]{1,0:T(8,128)} async-done(((f32[512,256]{1,0:T(8,128)}), f32[512,256]{1,0:T(8,128)}) %all-reduce.11.cloned.1.call-update) | async-done | bytes 524304 | tf_op jit(solution)/shard_map/psum | solution.py:73
  352.8 1.9 multiply_divide_fusion.2
  (28 shorter events, 2.1 us)
Async XLA Ops:
  7.2 143.1 %all-reduce.5.cloned.1.call-start = ((), (), s32[]{:S(2)}) async-start(), calls=%async_computation | async-start | bytes 2097152 | tf_op jit(solution)/shard_map/psum | solution.py:65
  7.9 48.7 %collective-permute-start = (f32[3072]{0:T(1024)S(1)}, f32[3072]{0:T(1024)S(1)}, u32[]{:S(2)}, u32[]{:S(2)}) collective-permute-start(f32[3072]{0:T(1024)S(1)} %slice.58), channel_id=1, source_target_pairs={{1,0},{2,1},{3,2},{4,3},{5,4},{6,5},{7,6},{9,8},{10,9},{11,10},{12... | collective-permute-start | bytes 36872 | tf_op jit(solution)/shard_map/ppermute | solution.py:17
  13.6 34.8 %copy-start = (f32[512,256]{1,0:T(8,128)S(1)}, f32[512,256]{1,0:T(8,128)}, u32[]{:S(2)}) copy-start(f32[512,256]{1,0:T(8,128)} %param.4) | copy-start | bytes 1572868
  13.6 34.8 %copy-start.1 = (f32[256,1024]{1,0:T(8,128)S(1)}, f32[256,1024]{1,0:T(8,128)}, u32[]{:S(2)}) copy-start(f32[256,1024]{1,0:T(8,128)} %param.5) | copy-start | bytes 3145732
  101.3 4.2 %copy-start.6 = (f32[512,1024]{1,0:T(8,128)S(1)}, f32[512,1024]{1,0:T(8,128)}, u32[]{:S(2)}) copy-start(f32[512,1024]{1,0:T(8,128)} %fusion.30) | copy-start | bytes 6291460
  104.1 1.4 copy-start.2
  110.0 120.0 %all-reduce.7.cloned.1.call-start = ((), (), s32[]{:S(2)}) async-start(), calls=%async_computation.1 | async-start | bytes 1048576 | tf_op jit(solution)/shard_map/psum | solution.py:73
  150.3 3.5 copy-start.3
  156.5 116.8 %all-reduce.9.cloned.1.call-start = ((), (), s32[]{:S(2)}) async-start(), calls=%async_computation.2 | async-start | bytes 2097152 | tf_op jit(solution)/shard_map/psum | solution.py:65
  229.9 3.2 copy-start.4
  237.6 115.2 %all-reduce.11.cloned.1.call-start = ((), (), s32[]{:S(2)}) async-start(), calls=%async_computation.3 | async-start | bytes 1048576 | tf_op jit(solution)/shard_map/psum | solution.py:73
  273.2 3.5 copy-start.5
Sparse Core Ops, SparseCore 0:
  110.1 40.1 all-reduce.4
  156.6 73.2 all-reduce.6
  237.7 35.4 all-reduce.8
  279.6 73.2 all-reduce.10
where the time goes:
time: 362 us; the launch traced here: 361 us
  waiting for transfers between devices  164 us (45%)
  blocking collectives  56.9 us (16%)
  other arithmetic  44.2 us (12%)
  matrix products  43.2 us (12%)
  local copies, waits for them, and re-layouts  37.6 us (10%)
  between operations  13.9 us (4%)
    psum x2, waiting for transfers between devices, local(): spectral, row_sums = lax.psum((spectral, row_sums), 'tm')  103 us
    psum x2, waiting for transfers between devices, local(): numer, column_sums = lax.psum((numer, column_sums), 'freq')  61.4 us
    psum x2, blocking collectives, local(): spectral, row_sums = lax.psum((spectral, row_sums), 'tm')  42.8 us
    another operation x1, other arithmetic  34.8 us
    slice x5, local copies, waits for them, and re-layouts, cut_frames(): blocks[j:j + count]  29 us
    dot_general x1, matrix products, spectrum(): jnp.einsum('wc,fw->cf', table, windowed, preferred_element_type=jnp.float32)  20.1 us
    psum x2, blocking collectives, local(): numer, column_sums = lax.psum((numer, column_sums), 'freq')  14 us
    dot_general x2, matrix products, local(): jnp.einsum('kr,kf->rf', factor_w, ratio, precision=lax.Precision.HIGHEST)  8.9 us
  transfers between devices with their start and end apart: 5, of which 4 were waited for; matrix products, arithmetic and copies ran while one was open for 14% of the time, Pallas kernels for 0%

commit v1 on v0

--- a/solution.py
+++ b/solution.py
@@ -9,6 +9,7 @@
 HOP = 1024
 K = 2048
 ITERS = 2
+HI = lax.Precision.HIGHEST
 
 
 def shifted(value, axis, by):
@@ -43,6 +44,54 @@
     return (real_part * real_part + imag_part * imag_part) / (0.375 * WIN)
 
 
+def halves(x, dim, bit):
+    lo, hi = jnp.split(x, 2, axis=dim)
+    keep = jnp.where(bit == 0, lo, hi)
+    send = jnp.where(bit == 0, hi, lo)
+    return keep, send
+
+
+def reduce_scatter(x, extra, axis, dim):
+    n = lax.axis_size(axis)
+    idx = lax.axis_index(axis)
+    d = 1
+    while d < n:
+        bit = (idx // d) % 2
+        keep, send = halves(x, dim, bit)
+        pairs = [(i, i ^ d) for i in range(n)]
+        got, got_extra = lax.ppermute((send, extra), axis, pairs)
+        x = keep + got
+        extra = extra + got_extra
+        d *= 2
+    return x, extra
+
+
+def chunk_of(x, axis, dim):
+    n = lax.axis_size(axis)
+    idx = lax.axis_index(axis)
+    d = 1
+    while d < n:
+        bit = (idx // d) % 2
+        x, _ = halves(x, dim, bit)
+        d *= 2
+    return x
+
+
+def all_gather(x, axis, dim):
+    n = lax.axis_size(axis)
+    idx = lax.axis_index(axis)
+    d = n // 2
+    while d >= 1:
+        bit = (idx // d) % 2
+        pairs = [(i, i ^ d) for i in range(n)]
+        got = lax.ppermute(x, axis, pairs)
+        first = jnp.where(bit == 0, x, got)
+        second = jnp.where(bit == 0, got, x)
+        x = jnp.concatenate([first, second], axis=dim)
+        d //= 2
+    return x
+
+
 def local(signal, w_init, h_init):
     steps_per = WIN // HOP
     frames_dev = signal.shape[0] // HOP
@@ -56,22 +105,22 @@
     factor_w = w_init
     factor_h = h_init
     for step in range(ITERS):
-        model = jnp.dot(
-            factor_w, factor_h, precision=lax.Precision.HIGHEST, preferred_element_type=jnp.float32
-        )
+        model = jnp.dot(factor_w, factor_h, precision=HI, preferred_element_type=jnp.float32)
         ratio = power / model
-        numer = jnp.einsum("kr,kf->rf", factor_w, ratio, precision=lax.Precision.HIGHEST)
+        numer = jnp.einsum("kr,kf->rf", factor_w, ratio, precision=HI)
         column_sums = jnp.sum(factor_w, axis=0)
-        numer, column_sums = lax.psum((numer, column_sums), "freq")
-        factor_h = factor_h * numer / column_sums[:, None]
-        model = jnp.dot(
-            factor_w, factor_h, precision=lax.Precision.HIGHEST, preferred_element_type=jnp.float32
-        )
+        numer, column_sums = reduce_scatter(numer, column_sums, "freq", 1)
+        h_part = chunk_of(factor_h, "freq", 1)
+        h_part = h_part * numer / column_sums[:, None]
+        factor_h = all_gather(h_part, "freq", 1)
+        model = jnp.dot(factor_w, factor_h, precision=HI, preferred_element_type=jnp.float32)
         ratio = power / model
         row_sums = jnp.sum(factor_h, axis=1)
-        spectral = jnp.einsum("kf,rf->kr", ratio, factor_h, precision=lax.Precision.HIGHEST)
-        spectral, row_sums = lax.psum((spectral, row_sums), "tm")
-        factor_w = factor_w * spectral / row_sums[None, :]
+        spectral = jnp.einsum("kf,rf->kr", ratio, factor_h, precision=HI)
+        spectral, row_sums = reduce_scatter(spectral, row_sums, "tm", 0)
+        w_part = chunk_of(factor_w, "tm", 0)
+        w_part = w_part * spectral / row_sums[None, :]
+        factor_w = all_gather(w_part, "tm", 0)
     return (factor_w, factor_h)
 
 

time: 362 us -> 245 us (0.68)
  waiting for transfers between devices: 164 us -> 91 us
  blocking collectives: 56.9 us -> 0 us
  starting transfers between devices: 1.44 us -> 27.8 us
  between operations: 13.9 us -> 1.13 us
    psum x4 -> x0, waiting for transfers between devices: 164 us -> none  [the longest x2 103 us: local(): spectral, row_sums = lax.psum((spectral, row_sums), 'tm')]
    ppermute x0 -> x30, waiting for transfers between devices: none -> 91 us  [the longest x10 45.9 us: all_gather(): got = lax.ppermute(x, axis, pairs)]
    psum x4 -> x0, blocking collectives: 56.9 us -> none  [the longest x2 42.8 us: local(): spectral, row_sums = lax.psum((spectral, row_sums), 'tm')]
    ppermute x0 -> x30, starting transfers between devices: none -> 26.5 us  [the longest x20 21.7 us: reduce_scatter(): got, got_extra = lax.ppermute((send, extra), axis, pairs)]
    unnamed x17 -> x14, local copies, waits for them, and re-layouts: 7.39 us -> 7.19 us
  transfers between devices with their start and end apart: 5 -> 31, of which waited for: 4 -> 23; matrix products, arithmetic and copies ran while one was open for 14% -> 22% of each run, Pallas kernels for 0% -> 0%
where the time goes in v1:
time: 245 us; the launch traced here: 244 us
  waiting for transfers between devices  91 us (37%)
  matrix products  43 us (18%)
  other arithmetic  42.4 us (17%)
  local copies, waits for them, and re-layouts  38.5 us (16%)
  starting transfers between devices  27.8 us (11%)
    ppermute x10, waiting for transfers between devices, all_gather(): got = lax.ppermute(x, axis, pairs)  45.9 us
    ppermute x20, waiting for transfers between devices, reduce_scatter(): got, got_extra = lax.ppermute((send, extra), axis, pairs)  45.2 us
    another operation x1, other arithmetic  34.8 us
    slice x5, local copies, waits for them, and re-layouts, cut_frames(): blocks[j:j + count]  29.1 us
    ppermute x20, starting transfers between devices, reduce_scatter(): got, got_extra = lax.ppermute((send, extra), axis, pairs)  21.7 us
    dot_general x1, matrix products, spectrum(): jnp.einsum('wc,fw->cf', table, windowed, preferred_element_type=jnp.float32)  20.1 us
    dot_general x4, matrix products, local(): jnp.dot(factor_w, factor_h, precision=HI, preferred_element_type=jnp.floa...  9.02 us
    dot_general x2, matrix products, local(): numer = jnp.einsum('kr,kf->rf', factor_w, ratio, precision=HI)  8.56 us
  transfers between devices with their start and end apart: 31, of which 23 were waited for; matrix products, arithmetic and copies ran while one was open for 22% of the time, Pallas kernels for 0%

profile of v1, /device:TPU:0, one launch (start us, length us, event | category | flops | bytes accessed | tf_op | source)
XLA Modules:
  0.0 243.9 jit_solution(7807783347791501447)
XLA Ops:
  2.6 4.4 %constant_dynamic-update-slice_fusion.1 = f32[1051648]{0:T(1024)} fusion(f32[1048576]{0:T(1024)} %param.3), kind=kLoop, calls=%fused_computation.99 | loop fusion | bytes 8388608
  7.0 34.8 %cosine_convert_fusion = (bf16[4096,512]{1,0:T(8,128)(2,1)}, bf16[4096,512]{1,0:T(8,128)(2,1)}) fusion(s32[512]{0:T(512)S(1)} %iota_add_fusion), kind=kLoop, calls=%fused_computation.13 | loop fusion | flops 33554432 | bytes 8390656 | tf_op jit(solution)/shard_map/convert
  41.9 3.2 %fusion.48 = f32[512,1024]{1,0:T(8,128)} fusion(f32[512,256]{1,0:T(8,128)S(1)} %copy-done, f32[256,1024]{1,0:T(8,128)S(1)} %copy-done.1), kind=kOutput, calls=%fused_computation.114 | convolution fusion | flops 1610612736 | bytes 3670016 | tf_op jit(solution)/shard_map/dot_general | solution.py:108
  45.1 4.9 %slice.57 = f32[1024,1024]{1,0:T(8,128)} reshape(f32[1048576]{0:T(1024)} %param.3) | data formatting | bytes 8388608 | tf_op jit(solution)/shard_map/slice | solution.py:36
  50.6 9.5 %fusion.46 = (f32[1048576]{0:T(1024)}, f32[1048576]{0:T(1024)}, f32[1048576]{0:T(1024)}) fusion(f32[1051648]{0:T(1024)} %constant_dynamic-update-slice_fusion), kind=kLoop, calls=%fused_computation.112 | loop fusion | bytes 25165824 | tf_op jit(solution)/shard_map/slice | solution.py:36
  60.1 4.9 %slice.60 = f32[1024,1024]{1,0:T(8,128)} reshape(f32[1048576]{0:T(1024)} %get-tuple-element.15) | data formatting | bytes 8388608 | tf_op jit(solution)/shard_map/slice | solution.py:36
  64.9 4.9 %slice.62 = f32[1024,1024]{1,0:T(8,128)} reshape(f32[1048576]{0:T(1024)} %get-tuple-element.17) | data formatting | bytes 8388608 | tf_op jit(solution)/shard_map/slice | solution.py:36
  69.8 5.0 %slice.64 = f32[1024,1024]{1,0:T(8,128)} reshape(f32[1048576]{0:T(1024)} %get-tuple-element.16) | data formatting | bytes 8388608 | tf_op jit(solution)/shard_map/slice | solution.py:36
  74.8 20.1 %fusion.4 = f32[1024,1024]{1,0:T(8,128)} fusion(bf16[4096,512]{1,0:T(8,128)(2,1)} %get-tuple-element.39, bf16[4096,512]{1,0:T(8,128)(2,1)} %get-tuple-element.38, f32[1024,1024]{1,0:T(8,128)} %slice.64, f32[1024,1024]{1,0:T(8,128)} %slice.62, f32[1024,1024]{1,0:T(8,128)} %slice.60, f32[1024,1024]{1,0:T(8,128)} %slice.57, f32[4096]{0:T(1024)S(1)} %multiply_subtract_fusion), kind=kOutput, calls=%fused_computation.8 | convolution fusion | flops 8627683328 | bytes 29376512 | tf_op jit(solution)/shard_map/wc,fw->cf/dot_general | solution.py:41
  94.9 2.8 %fusion.13 = f32[512,1024]{1,0:T(8,128)S(1)} fusion(f32[1024,1024]{1,0:T(8,128)} %fusion.4), kind=kLoop, calls=%fused_computation.19 | loop fusion | flops 2097152 | bytes 6291456 | tf_op jit(solution)/shard_map/div | solution.py:44
  97.7 3.5 %fusion.21 = f32[256,1024]{0,1:T(8,128)S(1)} fusion(f32[512,256]{1,0:T(8,128)S(1)} %copy-done, f32[512,1024]{1,0:T(8,128)S(1)} %fusion.13, f32[512,1024]{1,0:T(8,128)S(1)} %copy-done.4), kind=kOutput, calls=%fused_computation.29 | convolution fusion | flops 1611137024 | bytes 5767168 | tf_op jit(solution)/shard_map/kr,kf->rf/dot_general | solution.py:110
  105.1 3.0 %collective-permute-start.4 = (f32[256]{0:T(256)S(1)}, f32[256]{0:T(256)S(1)}, u32[]{:S(2)}, u32[]{:S(2)}) collective-permute-start(f32[256]{0:T(256)S(1)} %add.136), channel_id=1, source_target_pairs={{0,16},{8,24},{16,0},{24,8},{1,17},{9,25},{17,1},{25,9},{2,18},{10... | collective-permute-start | bytes 3080 | tf_op jit(solution)/shard_map/ppermute | solution.py:62
  109.6 7.7 %collective-permute-done.2 = f32[256,256]{0,1:T(8,128)S(1)} collective-permute-done((f32[256,256]{0,1:T(8,128)S(1)}, f32[256,256]{0,1:T(8,128)S(1)}, u32[]{:S(2)}, u32[]{:S(2)}) %collective-permute-start.2) | collective-permute-done | bytes 262176 | tf_op jit(solution)/shard_map/ppermute | solution.py:62
  117.8 6.8 %collective-permute-done.5 = f32[256,256]{0,1:T(8,128)S(1)} collective-permute-done((f32[256,256]{0,1:T(8,128)S(1)}, f32[256,256]{0,1:T(8,128)S(1)}, u32[]{:S(2)}, u32[]{:S(2)}) %collective-permute-start.5) | collective-permute-done | bytes 262176 | tf_op jit(solution)/shard_map/ppermute | solution.py:87
  128.6 3.5 %fusion.14 = f32[512,256]{1,0:T(8,128)S(1)} fusion(f32[512,1024]{1,0:T(8,128)} %copy-done.2, f32[1024,512]{0,1:T(8,128)S(1)} %fusion.25, f32[256,512]{0,1:T(8,128)S(1)} %get-tuple-element.14, f32[256,512]{0,1:T(8,128)S(1)} %get-tuple-element.13), kind=kOutput, calls=%fused_computation.22 | convolution fusion | flops 1611399168 | bytes 5767168 | tf_op jit(solution)/shard_map/kf,rf->kr/dot_general | solution.py:119
  132.2 2.7 %collective-permute-start.7 = (f32[256,256]{1,0:T(8,128)S(1)}, f32[256,256]{1,0:T(8,128)S(1)}, u32[]{:S(2)}, u32[]{:S(2)}) collective-permute-start(f32[256,256]{1,0:T(8,128)S(1)} %slice_select_fusion.7), channel_id=1, source_target_pairs={{0,1},{1,0},{2,3},{3,2},{4,5},{5,4},{6,7},{7,6},{8,9},{9,8},{10,11... | collective-permute-start | bytes 786440 | tf_op jit(solution)/shard_map/ppermute | solution.py:62
  135.2 6.3 %collective-permute-done.7 = f32[256,256]{1,0:T(8,128)S(1)} collective-permute-done((f32[256,256]{1,0:T(8,128)S(1)}, f32[256,256]{1,0:T(8,128)S(1)}, u32[]{:S(2)}, u32[]{:S(2)}) %collective-permute-start.7) | collective-permute-done | bytes 262176 | tf_op jit(solution)/shard_map/ppermute | solution.py:62
  141.6 2.8 %collective-permute-start.8 = (f32[128,256]{1,0:T(8,128)S(1)}, f32[128,256]{1,0:T(8,128)S(1)}, u32[]{:S(2)}, u32[]{:S(2)}) collective-permute-start(f32[128,256]{1,0:T(8,128)S(1)} %slice_select_fusion.12), channel_id=1, source_target_pairs={{0,2},{1,3},{2,0},{3,1},{4,6},{5,7},{6,4},{7,5},{8,10},{9,11},{10,... | collective-permute-start | bytes 393224 | tf_op jit(solution)/shard_map/ppermute | solution.py:62
  144.5 3.5 %collective-permute-done.11 = f32[256]{0:T(256)S(1)} collective-permute-done((f32[256]{0:T(256)S(1)}, f32[256]{0:T(256)S(1)}, u32[]{:S(2)}, u32[]{:S(2)}) %collective-permute-start.11) | collective-permute-done | bytes 1056 | tf_op jit(solution)/shard_map/ppermute | solution.py:62
  148.1 2.6 %collective-permute-start.12 = (f32[256]{0:T(256)S(1)}, f32[256]{0:T(256)S(1)}, u32[]{:S(2)}, u32[]{:S(2)}) collective-permute-start(f32[256]{0:T(256)S(1)} %add.142), channel_id=1, source_target_pairs={{0,4},{1,5},{2,6},{3,7},{4,0},{5,1},{6,2},{7,3},{8,12},{9,13},{10,... | collective-permute-start | bytes 3080 | tf_op jit(solution)/shard_map/ppermute | solution.py:62
  152.5 3.4 %collective-permute-done.9 = f32[64,256]{1,0:T(8,128)S(1)} collective-permute-done((f32[64,256]{1,0:T(8,128)S(1)}, f32[64,256]{1,0:T(8,128)S(1)}, u32[]{:S(2)}, u32[]{:S(2)}) %collective-permute-start.9) | collective-permute-done | bytes 65568 | tf_op jit(solution)/shard_map/ppermute | solution.py:62
  156.5 4.8 %collective-permute-done.13 = f32[64,256]{1,0:T(8,128)S(1)} collective-permute-done((f32[64,256]{1,0:T(8,128)S(1)}, f32[64,256]{1,0:T(8,128)S(1)}, u32[]{:S(2)}, u32[]{:S(2)}) %collective-permute-start.13) | collective-permute-done | bytes 65568 | tf_op jit(solution)/shard_map/ppermute | solution.py:87
  162.7 3.6 %collective-permute-done.14 = f32[128,256]{1,0:T(8,128)S(1)} collective-permute-done((f32[128,256]{1,0:T(8,128)S(1)}, f32[128,256]{1,0:T(8,128)S(1)}, u32[]{:S(2)}, u32[]{:S(2)}) %collective-permute-start.14) | collective-permute-done | bytes 131104 | tf_op jit(solution)/shard_map/ppermute | solution.py:87
  167.0 5.8 %collective-permute-done.15 = f32[256,256]{1,0:T(8,128)S(1)} collective-permute-done((f32[256,256]{1,0:T(8,128)S(1)}, f32[256,256]{1,0:T(8,128)S(1)}, u32[]{:S(2)}, u32[]{:S(2)}) %collective-permute-start.15) | collective-permute-done | bytes 262176 | tf_op jit(solution)/shard_map/ppermute | solution.py:87
  175.0 5.1 %fusion.17 = f32[256,1024]{0,1:T(8,128)S(1)} fusion(f32[512,1024]{1,0:T(8,128)} %copy-done.2, f32[512,1024]{1,0:T(8,128)S(1)} %fusion.24, f32[256,256]{1,0:T(8,128)S(1)} %get-tuple-element.9, f32[256,256]{1,0:T(8,128)S(1)} %get-tuple-element.27), kind=kOutput, calls=%fused_computation.25 | convolution fusion | flops 1611268096 | bytes 5767168 | tf_op jit(solution)/shard_map/kr,kf->rf/dot_general | solution.py:110
  185.6 5.2 %collective-permute-done.19 = f32[256]{0:T(256)S(1)} collective-permute-done((f32[256]{0:T(256)S(1)}, f32[256]{0:T(256)S(1)}, u32[]{:S(2)}, u32[]{:S(2)}) %collective-permute-start.19) | collective-permute-done | bytes 1056 | tf_op jit(solution)/shard_map/ppermute | solution.py:62
  191.5 6.9 %collective-permute-done.20 = f32[256,256]{0,1:T(8,128)S(1)} collective-permute-done((f32[256,256]{0,1:T(8,128)S(1)}, f32[256,256]{0,1:T(8,128)S(1)}, u32[]{:S(2)}, u32[]{:S(2)}) %collective-permute-start.20) | collective-permute-done | bytes 262176 | tf_op jit(solution)/shard_map/ppermute | solution.py:87
  206.5 6.4 %collective-permute-done.25 = f32[256]{0:T(256)S(1)} collective-permute-done((f32[256]{0:T(256)S(1)}, f32[256]{0:T(256)S(1)}, u32[]{:S(2)}, u32[]{:S(2)}) %collective-permute-start.25) | collective-permute-done | bytes 1056 | tf_op jit(solution)/shard_map/ppermute | solution.py:62
  221.3 4.9 %collective-permute-done.24 = f32[64,256]{1,0:T(8,128)S(1)} collective-permute-done((f32[64,256]{1,0:T(8,128)S(1)}, f32[64,256]{1,0:T(8,128)S(1)}, u32[]{:S(2)}, u32[]{:S(2)}) %collective-permute-start.24) | collective-permute-done | bytes 65568 | tf_op jit(solution)/shard_map/ppermute | solution.py:62
  226.6 4.8 %collective-permute-done.28 = f32[64,256]{1,0:T(8,128)S(1)} collective-permute-done((f32[64,256]{1,0:T(8,128)S(1)}, f32[64,256]{1,0:T(8,128)S(1)}, u32[]{:S(2)}, u32[]{:S(2)}) %collective-permute-start.28) | collective-permute-done | bytes 65568 | tf_op jit(solution)/shard_map/ppermute | solution.py:87
  231.6 5.0 %collective-permute-done.29 = f32[128,256]{1,0:T(8,128)S(1)} collective-permute-done((f32[128,256]{1,0:T(8,128)S(1)}, f32[128,256]{1,0:T(8,128)S(1)}, u32[]{:S(2)}, u32[]{:S(2)}) %collective-permute-start.29) | collective-permute-done | bytes 131104 | tf_op jit(solution)/shard_map/ppermute | solution.py:87
  238.6 4.4 %collective-permute-done.30 = f32[256,256]{1,0:T(8,128)S(1)} collective-permute-done((f32[256,256]{1,0:T(8,128)S(1)}, f32[256,256]{1,0:T(8,128)S(1)}, u32[]{:S(2)}, u32[]{:S(2)}) %collective-permute-start.30) | collective-permute-done | bytes 262176 | tf_op jit(solution)/shard_map/ppermute | solution.py:87
  (124 shorter events, 45.9 us)
Async XLA Ops:
  1.3 48.6 %collective-permute-start = (f32[3072]{0:T(1024)S(1)}, f32[3072]{0:T(1024)S(1)}, u32[]{:S(2)}, u32[]{:S(2)}) collective-permute-start(f32[3072]{0:T(1024)S(1)} %slice.58), channel_id=1, source_target_pairs={{1,0},{2,1},{3,2},{4,3},{5,4},{6,5},{7,6},{9,8},{10,9},{11,10},{12... | collective-permute-start | bytes 36872 | tf_op jit(solution)/shard_map/ppermute | solution.py:18
  7.0 34.8 %copy-start.1 = (f32[256,1024]{1,0:T(8,128)S(1)}, f32[256,1024]{1,0:T(8,128)}, u32[]{:S(2)}) copy-start(f32[256,1024]{1,0:T(8,128)} %param.5) | copy-start | bytes 3145732
  102.1 6.0 %collective-permute-start.1 = (f32[256,512]{0,1:T(8,128)}, f32[256,512]{0,1:T(8,128)}, u32[]{:S(2)}, u32[]{:S(2)}) collective-permute-start(f32[256,512]{0,1:T(8,128)} %slice_select_fusion.1), channel_id=1, source_target_pairs={{0,8},{8,0},{16,24},{24,16},{1,9},{9,1},{17,25},{25,17},{2,10},{10... | collective-permute-start | bytes 1572872 | tf_op jit(solution)/shard_map/ppermute | solution.py:62
  102.6 2.4 collective-permute-start.3
  105.1 4.6 %collective-permute-start.4 = (f32[256]{0:T(256)S(1)}, f32[256]{0:T(256)S(1)}, u32[]{:S(2)}, u32[]{:S(2)}) collective-permute-start(f32[256]{0:T(256)S(1)} %add.136), channel_id=1, source_target_pairs={{0,16},{8,24},{16,0},{24,8},{1,17},{9,25},{17,1},{25,9},{2,18},{10... | collective-permute-start | bytes 3080 | tf_op jit(solution)/shard_map/ppermute | solution.py:62
  109.3 8.0 %collective-permute-start.2 = (f32[256,256]{0,1:T(8,128)S(1)}, f32[256,256]{0,1:T(8,128)S(1)}, u32[]{:S(2)}, u32[]{:S(2)}) collective-permute-start(f32[256,256]{0,1:T(8,128)S(1)} %slice_select_fusion.8), channel_id=1, source_target_pairs={{0,16},{8,24},{16,0},{24,8},{1,17},{9,25},{17,1},{25,9},{2,18},{10... | collective-permute-start | bytes 786440 | tf_op jit(solution)/shard_map/ppermute | solution.py:62
  117.4 7.2 %collective-permute-start.5 = (f32[256,256]{0,1:T(8,128)S(1)}, f32[256,256]{0,1:T(8,128)S(1)}, u32[]{:S(2)}, u32[]{:S(2)}) collective-permute-start(f32[256,256]{0,1:T(8,128)S(1)} %fusion.30), channel_id=1, source_target_pairs={{0,16},{8,24},{16,0},{24,8},{1,17},{9,25},{17,1},{25,9},{2,18},{10... | collective-permute-start | bytes 786440 | tf_op jit(solution)/shard_map/ppermute | solution.py:87
  124.6 2.0 collective-permute-start.6
  132.2 9.3 %collective-permute-start.7 = (f32[256,256]{1,0:T(8,128)S(1)}, f32[256,256]{1,0:T(8,128)S(1)}, u32[]{:S(2)}, u32[]{:S(2)}) collective-permute-start(f32[256,256]{1,0:T(8,128)S(1)} %slice_select_fusion.7), channel_id=1, source_target_pairs={{0,1},{1,0},{2,3},{3,2},{4,5},{5,4},{6,7},{7,6},{8,9},{9,8},{10,11... | collective-permute-start | bytes 786440 | tf_op jit(solution)/shard_map/ppermute | solution.py:62
  135.1 9.3 %collective-permute-start.10 = (f32[256]{0:T(256)S(1)}, f32[256]{0:T(256)S(1)}, u32[]{:S(2)}, u32[]{:S(2)}) collective-permute-start(f32[256]{0:T(256)S(1)} %reduce_sum.63), channel_id=1, source_target_pairs={{0,1},{1,0},{2,3},{3,2},{4,5},{5,4},{6,7},{7,6},{8,9},{9,8},{10,11... | collective-permute-start | bytes 3080 | tf_op jit(solution)/shard_map/ppermute | solution.py:62
  141.6 9.1 %collective-permute-start.8 = (f32[128,256]{1,0:T(8,128)S(1)}, f32[128,256]{1,0:T(8,128)S(1)}, u32[]{:S(2)}, u32[]{:S(2)}) collective-permute-start(f32[128,256]{1,0:T(8,128)S(1)} %slice_select_fusion.12), channel_id=1, source_target_pairs={{0,2},{1,3},{2,0},{3,1},{4,6},{5,7},{6,4},{7,5},{8,10},{9,11},{10,... | collective-permute-start | bytes 393224 | tf_op jit(solution)/shard_map/ppermute | solution.py:62
  144.4 3.6 %collective-permute-start.11 = (f32[256]{0:T(256)S(1)}, f32[256]{0:T(256)S(1)}, u32[]{:S(2)}, u32[]{:S(2)}) collective-permute-start(f32[256]{0:T(256)S(1)} %add.141), channel_id=1, source_target_pairs={{0,2},{1,3},{2,0},{3,1},{4,6},{5,7},{6,4},{7,5},{8,10},{9,11},{10,... | collective-permute-start | bytes 3080 | tf_op jit(solution)/shard_map/ppermute | solution.py:62
  148.1 4.5 %collective-permute-start.12 = (f32[256]{0:T(256)S(1)}, f32[256]{0:T(256)S(1)}, u32[]{:S(2)}, u32[]{:S(2)}) collective-permute-start(f32[256]{0:T(256)S(1)} %add.142), channel_id=1, source_target_pairs={{0,4},{1,5},{2,6},{3,7},{4,0},{5,1},{6,2},{7,3},{8,12},{9,13},{10,... | collective-permute-start | bytes 3080 | tf_op jit(solution)/shard_map/ppermute | solution.py:62
  150.7 5.2 %collective-permute-start.9 = (f32[64,256]{1,0:T(8,128)S(1)}, f32[64,256]{1,0:T(8,128)S(1)}, u32[]{:S(2)}, u32[]{:S(2)}) collective-permute-start(f32[64,256]{1,0:T(8,128)S(1)} %slice_select_fusion.16), channel_id=1, source_target_pairs={{0,4},{1,5},{2,6},{3,7},{4,0},{5,1},{6,2},{7,3},{8,12},{9,13},{10,... | collective-permute-start | bytes 196616 | tf_op jit(solution)/shard_map/ppermute | solution.py:62
  156.0 5.3 %collective-permute-start.13 = (f32[64,256]{1,0:T(8,128)S(1)}, f32[64,256]{1,0:T(8,128)S(1)}, u32[]{:S(2)}, u32[]{:S(2)}) collective-permute-start(f32[64,256]{1,0:T(8,128)S(1)} %fusion.34), channel_id=1, source_target_pairs={{0,4},{1,5},{2,6},{3,7},{4,0},{5,1},{6,2},{7,3},{8,12},{9,13},{10,... | collective-permute-start | bytes 196616 | tf_op jit(solution)/shard_map/ppermute | solution.py:87
  161.3 5.0 %collective-permute-start.14 = (f32[128,256]{1,0:T(8,128)S(1)}, f32[128,256]{1,0:T(8,128)S(1)}, u32[]{:S(2)}, u32[]{:S(2)}) collective-permute-start(f32[128,256]{1,0:T(8,128)S(1)} %pad_maximum_fusion.14), channel_id=1, source_target_pairs={{0,2},{1,3},{2,0},{3,1},{4,6},{5,7},{6,4},{7,5},{8,10},{9,11},{10,... | collective-permute-start | bytes 393224 | tf_op jit(solution)/shard_map/ppermute | solution.py:87
  166.4 6.4 %collective-permute-start.15 = (f32[256,256]{1,0:T(8,128)S(1)}, f32[256,256]{1,0:T(8,128)S(1)}, u32[]{:S(2)}, u32[]{:S(2)}) collective-permute-start(f32[256,256]{1,0:T(8,128)S(1)} %pad_maximum_fusion.12), channel_id=1, source_target_pairs={{0,1},{1,0},{2,3},{3,2},{4,5},{5,4},{6,7},{7,6},{8,9},{9,8},{10,11... | collective-permute-start | bytes 786440 | tf_op jit(solution)/shard_map/ppermute | solution.py:87
  180.2 2.0 collective-permute-start.16
  182.3 8.5 %collective-permute-start.17 = (f32[256,256]{0,1:T(8,128)S(1)}, f32[256,256]{0,1:T(8,128)S(1)}, u32[]{:S(2)}, u32[]{:S(2)}) collective-permute-start(f32[256,256]{0,1:T(8,128)S(1)} %slice_select_fusion.6), channel_id=1, source_target_pairs={{0,16},{8,24},{16,0},{24,8},{1,17},{9,25},{17,1},{25,9},{2,18},{10... | collective-permute-start | bytes 786440 | tf_op jit(solution)/shard_map/ppermute | solution.py:62
  182.9 1.2 collective-permute-start.18
  184.1 6.7 %collective-permute-start.19 = (f32[256]{0:T(256)S(1)}, f32[256]{0:T(256)S(1)}, u32[]{:S(2)}, u32[]{:S(2)}) collective-permute-start(f32[256]{0:T(256)S(1)} %add.146), channel_id=1, source_target_pairs={{0,16},{8,24},{16,0},{24,8},{1,17},{9,25},{17,1},{25,9},{2,18},{10... | collective-permute-start | bytes 3080 | tf_op jit(solution)/shard_map/ppermute | solution.py:62
  190.9 7.5 %collective-permute-start.20 = (f32[256,256]{0,1:T(8,128)S(1)}, f32[256,256]{0,1:T(8,128)S(1)}, u32[]{:S(2)}, u32[]{:S(2)}) collective-permute-start(f32[256,256]{0,1:T(8,128)S(1)} %fusion.28), channel_id=1, source_target_pairs={{0,16},{8,24},{16,0},{24,8},{1,17},{9,25},{17,1},{25,9},{2,18},{10... | collective-permute-start | bytes 786440 | tf_op jit(solution)/shard_map/ppermute | solution.py:87
  198.5 2.0 collective-permute-start.21
  204.4 9.8 %collective-permute-start.22 = (f32[256,256]{1,0:T(8,128)S(1)}, f32[256,256]{1,0:T(8,128)S(1)}, u32[]{:S(2)}, u32[]{:S(2)}) collective-permute-start(f32[256,256]{1,0:T(8,128)S(1)} %slice_select_fusion.5), channel_id=1, source_target_pairs={{0,1},{1,0},{2,3},{3,2},{4,5},{5,4},{6,7},{7,6},{8,9},{9,8},{10,11... | collective-permute-start | bytes 786440 | tf_op jit(solution)/shard_map/ppermute | solution.py:62
  205.1 7.8 %collective-permute-start.25 = (f32[256]{0:T(256)S(1)}, f32[256]{0:T(256)S(1)}, u32[]{:S(2)}, u32[]{:S(2)}) collective-permute-start(f32[256]{0:T(256)S(1)} %reduce_sum.69), channel_id=1, source_target_pairs={{0,1},{1,0},{2,3},{3,2},{4,5},{5,4},{6,7},{7,6},{8,9},{9,8},{10,11... | collective-permute-start | bytes 3080 | tf_op jit(solution)/shard_map/ppermute | solution.py:62
  212.9 3.6 %collective-permute-start.26 = (f32[256]{0:T(256)S(1)}, f32[256]{0:T(256)S(1)}, u32[]{:S(2)}, u32[]{:S(2)}) collective-permute-start(f32[256]{0:T(256)S(1)} %add.151), channel_id=1, source_target_pairs={{0,2},{1,3},{2,0},{3,1},{4,6},{5,7},{6,4},{7,5},{8,10},{9,11},{10,... | collective-permute-start | bytes 3080 | tf_op jit(solution)/shard_map/ppermute | solution.py:62
  214.3 5.0 %collective-permute-start.23 = (f32[128,256]{1,0:T(8,128)S(1)}, f32[128,256]{1,0:T(8,128)S(1)}, u32[]{:S(2)}, u32[]{:S(2)}) collective-permute-start(f32[128,256]{1,0:T(8,128)S(1)} %slice_select_fusion.11), channel_id=1, source_target_pairs={{0,2},{1,3},{2,0},{3,1},{4,6},{5,7},{6,4},{7,5},{8,10},{9,11},{10,... | collective-permute-start | bytes 393224 | tf_op jit(solution)/shard_map/ppermute | solution.py:62
  216.5 4.8 %collective-permute-start.27 = (f32[256]{0:T(256)S(1)}, f32[256]{0:T(256)S(1)}, u32[]{:S(2)}, u32[]{:S(2)}) collective-permute-start(f32[256]{0:T(256)S(1)} %add.152), channel_id=1, source_target_pairs={{0,4},{1,5},{2,6},{3,7},{4,0},{5,1},{6,2},{7,3},{8,12},{9,13},{10,... | collective-permute-start | bytes 3080 | tf_op jit(solution)/shard_map/ppermute | solution.py:62
  219.4 6.8 %collective-permute-start.24 = (f32[64,256]{1,0:T(8,128)S(1)}, f32[64,256]{1,0:T(8,128)S(1)}, u32[]{:S(2)}, u32[]{:S(2)}) collective-permute-start(f32[64,256]{1,0:T(8,128)S(1)} %slice_select_fusion.15), channel_id=1, source_target_pairs={{0,4},{1,5},{2,6},{3,7},{4,0},{5,1},{6,2},{7,3},{8,12},{9,13},{10,... | collective-permute-start | bytes 196616 | tf_op jit(solution)/shard_map/ppermute | solution.py:62
  226.2 5.3 %collective-permute-start.28 = (f32[64,256]{1,0:T(8,128)S(1)}, f32[64,256]{1,0:T(8,128)S(1)}, u32[]{:S(2)}, u32[]{:S(2)}) collective-permute-start(f32[64,256]{1,0:T(8,128)S(1)} %fusion.32), channel_id=1, source_target_pairs={{0,4},{1,5},{2,6},{3,7},{4,0},{5,1},{6,2},{7,3},{8,12},{9,13},{10,... | collective-permute-start | bytes 196616 | tf_op jit(solution)/shard_map/ppermute | solution.py:87
  231.5 5.0 %collective-permute-start.29 = (f32[128,256]{1,0:T(8,128)S(1)}, f32[128,256]{1,0:T(8,128)S(1)}, u32[]{:S(2)}, u32[]{:S(2)}) collective-permute-start(f32[128,256]{1,0:T(8,128)S(1)} %pad_maximum_fusion.15), channel_id=1, source_target_pairs={{0,2},{1,3},{2,0},{3,1},{4,6},{5,7},{6,4},{7,5},{8,10},{9,11},{10,... | collective-permute-start | bytes 393224 | tf_op jit(solution)/shard_map/ppermute | solution.py:87
  236.6 6.4 %collective-permute-start.30 = (f32[256,256]{1,0:T(8,128)S(1)}, f32[256,256]{1,0:T(8,128)S(1)}, u32[]{:S(2)}, u32[]{:S(2)}) collective-permute-start(f32[256,256]{1,0:T(8,128)S(1)} %pad_maximum_fusion.13), channel_id=1, source_target_pairs={{0,1},{1,0},{2,3},{3,2},{4,5},{5,4},{6,7},{7,6},{8,9},{9,8},{10,11... | collective-permute-start | bytes 786440 | tf_op jit(solution)/shard_map/ppermute | solution.py:87
  (4 other events, 53.6 us)

commit v2 on v1

--- a/solution.py
+++ b/solution.py
@@ -1,8 +1,12 @@
 import math
+
+import functools
 
 import jax
 import jax.numpy as jnp
 from jax import lax
+from jax.experimental import pallas as pl
+from jax.experimental.pallas import tpu as pltpu
 from jax.sharding import PartitionSpec as P
 
 WIN = 4096
@@ -18,30 +22,78 @@
     return lax.ppermute(value, axis, pairs)
 
 
-def dft_table(first, count):
-    samples = jnp.arange(WIN, dtype=jnp.int32)
-    bins = first + jnp.arange(count, dtype=jnp.int32)
-    phase = samples[:, None] * bins[None, :] % WIN
-    angle = phase.astype(jnp.float32) * (2.0 * math.pi / WIN)
-    return jnp.concatenate([jnp.cos(angle), jnp.sin(angle)], axis=1).astype(jnp.bfloat16)
-
-
 def hann_window():
     samples = jnp.arange(WIN, dtype=jnp.int32).astype(jnp.float32)
     return 0.5 - 0.5 * jnp.cos(samples * (2.0 * math.pi / WIN))
 
 
-def cut_frames(blocks, count):
-    steps_per = WIN // HOP
-    frames = jnp.concatenate([blocks[j : j + count] for j in range(steps_per)], axis=1)
-    return (frames * hann_window()[None, :]).astype(jnp.bfloat16)
+SUB = 128
 
 
-def spectrum(windowed, table, count):
-    both = jnp.einsum("wc,fw->cf", table, windowed, preferred_element_type=jnp.float32)
-    real_part = both[:count]
-    imag_part = both[count:]
-    return (real_part * real_part + imag_part * imag_part) / (0.375 * WIN)
+def small_tables(first, count):
+    bins = first + jnp.arange(count, dtype=jnp.int32)
+    a = jnp.arange(WIN // SUB, dtype=jnp.int32)
+    b = jnp.arange(SUB, dtype=jnp.int32)
+    pa = (a[:, None] * SUB * bins[None, :]) % WIN
+    pb = (b[:, None] * bins[None, :]) % WIN
+    sc = 2.0 * math.pi / WIN
+    ta = pa.astype(jnp.float32) * sc
+    tb = pb.astype(jnp.float32) * sc
+    return jnp.cos(ta), jnp.sin(ta), jnp.cos(tb), jnp.sin(tb)
+
+
+def dft_kernel(sig_hbm, tail_ref, win_ref, ca_ref, sa_ref, cb_ref, sb_ref, out_ref,
+               blocks, tab, acc_ref, sem, *, tf, count, frames):
+    i = pl.program_id(0)
+
+    @pl.when(i == 0)
+    def _():
+        copy = pltpu.make_async_copy(sig_hbm, blocks.at[pl.ds(0, frames), :], sem)
+        copy.start()
+        blocks[pl.ds(frames, 8), :] = tail_ref[...]
+        cb = cb_ref[...]
+        sb = sb_ref[...]
+        for a in range(WIN // SUB):
+            ca = ca_ref[a:a + 1, :]
+            sa = sa_ref[a:a + 1, :]
+            tab[pl.ds(a * SUB, SUB), pl.ds(0, count)] = (ca * cb - sa * sb).astype(jnp.bfloat16)
+            tab[pl.ds(a * SUB, SUB), pl.ds(count, count)] = (sa * cb + ca * sb).astype(jnp.bfloat16)
+        copy.wait()
+
+    base = pl.multiple_of(i * tf, tf)
+    rows = blocks[pl.ds(base, tf + 8), :]
+    for j in range(WIN // HOP):
+        x = (rows[j:j + tf, :] * win_ref[j:j + 1, :]).astype(jnp.bfloat16)
+        part = jnp.dot(x, tab[pl.ds(j * HOP, HOP), :], preferred_element_type=jnp.float32)
+        if j == 0:
+            acc_ref[...] = part
+        else:
+            acc_ref[...] += part
+    re = acc_ref[:, :count]
+    im = acc_ref[:, count:]
+    out_ref[...] = ((re * re + im * im) / (0.375 * WIN)).T
+
+
+def power_kernel(sig2d, tail8, win4, tables, count, tf=512, interpret=False):
+    frames = sig2d.shape[0]
+    ca, sa, cb, sb = tables
+    full = lambda shape: pl.BlockSpec(shape, lambda i: (0, 0), pipeline_mode=pl.Buffered(1))
+    return pl.pallas_call(
+        functools.partial(dft_kernel, tf=tf, count=count, frames=frames),
+        grid=(frames // tf,),
+        in_specs=[pl.BlockSpec(memory_space=pl.ANY),
+                  full(tail8.shape), full(win4.shape), full(ca.shape), full(sa.shape),
+                  full(cb.shape), full(sb.shape)],
+        out_specs=pl.BlockSpec((count, tf), lambda i: (0, i)),
+        out_shape=jax.ShapeDtypeStruct((count, frames), jnp.float32),
+        scratch_shapes=[pltpu.VMEM((frames + 8, HOP), jnp.float32),
+                        pltpu.VMEM((WIN, 2 * count), jnp.bfloat16),
+                        pltpu.VMEM((tf, 2 * count), jnp.float32),
+                        pltpu.SemaphoreType.DMA],
+        compiler_params=pltpu.CompilerParams(vmem_limit_bytes=48 * 1024 * 1024,
+                                             dimension_semantics=("arbitrary",)),
+        interpret=interpret,
+    )(sig2d, tail8, win4, ca, sa, cb, sb)
 
 
 def halves(x, dim, bit):
@@ -96,12 +148,11 @@
     steps_per = WIN // HOP
     frames_dev = signal.shape[0] // HOP
     tail = shifted(signal[: (steps_per - 1) * HOP], "tm", -1)
-    blocks = jnp.concatenate([signal, tail]).reshape(frames_dev + steps_per - 1, HOP)
+    tail8 = jnp.concatenate([tail, jnp.zeros(((8 - steps_per + 1) * HOP,), jnp.float32)])
     local_bins = K // lax.axis_size("freq")
-    windowed = cut_frames(blocks, frames_dev)
-    power = spectrum(
-        windowed, dft_table(lax.axis_index("freq") * local_bins, local_bins), local_bins
-    )
+    win4 = hann_window().reshape(steps_per, HOP)
+    tables = small_tables(lax.axis_index("freq") * local_bins, local_bins)
+    power = power_kernel(signal.reshape(frames_dev, HOP), tail8.reshape(8, HOP), win4, tables, local_bins)
     factor_w = w_init
     factor_h = h_init
     for step in range(ITERS):

time: 245 us -> 179 us (0.73)
  other arithmetic: 42.4 us -> 13.8 us
  local copies, waits for them, and re-layouts: 38.5 us -> 14.2 us
  matrix products: 43 us -> 21.3 us
  Pallas kernels: 0 us -> 12 us
  waiting for transfers between devices: 91 us -> 87.7 us
    another operation x1 -> x0, other arithmetic: 34.8 us -> none
    slice x5 -> x0, local copies, waits for them, and re-layouts: 29.1 us -> none  [cut_frames(): blocks[j:j + count]]
    dot_general x1 -> x0, matrix products: 20.1 us -> none  [spectrum(): jnp.einsum('wc,fw->cf', table, windowed, preferred_element_type=jnp.float32)]
    pallas_call x0 -> x1, Pallas kernels: none -> 12 us  [power_kernel(): pl.pallas_call(functools.partial(dft_kernel, tf=tf, count=count, frames=f...]
    reshape x0 -> x2, local copies, waits for them, and re-layouts: none -> 4.91 us  [the longest x1 4.9 us: local(): signal.reshape(frames_dev, HOP)]
    select_n x6, other arithmetic: 0.29 us -> 3.84 us  [halves(): keep = jnp.where(bit == 0, lo, hi)]
    div x1 -> x0, other arithmetic: 2.82 us -> none  [spectrum(): return (real_part * real_part + imag_part * imag_part) / (0.375 * WIN)]
    unnamed x14 -> x21, local copies, waits for them, and re-layouts: 7.19 us -> 6.34 us
  transfers between devices with their start and end apart: 31 -> 31, of which waited for: 23 -> 23; matrix products, arithmetic and copies ran while one was open for 22% -> 14% of each run, Pallas kernels for 0% -> 0%
where the time goes in v2:
time: 179 us
  waiting for transfers between devices  87.7 us (49%)
  starting transfers between devices  28.4 us (16%)
  matrix products  21.3 us (12%)
  local copies, waits for them, and re-layouts  14.2 us (8%)
  other arithmetic  13.8 us (8%)
  Pallas kernels  12 us (7%)
    ppermute x10, waiting for transfers between devices, all_gather(): got = lax.ppermute(x, axis, pairs)  44.8 us
    ppermute x20, waiting for transfers between devices, reduce_scatter(): got, got_extra = lax.ppermute((send, extra), axis, pairs)  42.8 us
    ppermute x20, starting transfers between devices, reduce_scatter(): got, got_extra = lax.ppermute((send, extra), axis, pairs)  20.5 us
    pallas_call x1, Pallas kernels, power_kernel(): pl.pallas_call(functools.partial(dft_kernel, tf=tf, count=count, frames=f...  12 us
    dot_general x4, matrix products, local(): jnp.dot(factor_w, factor_h, precision=HI, preferred_element_type=jnp.floa...  10.5 us
    dot_general x2, matrix products, local(): numer = jnp.einsum('kr,kf->rf', factor_w, ratio, precision=HI)  6.96 us
    ppermute x10, starting transfers between devices, all_gather(): got = lax.ppermute(x, axis, pairs)  6.59 us
    unnamed x21, local copies, waits for them, and re-layouts  6.34 us
  transfers between devices with their start and end apart: 31, of which 23 were waited for; matrix products, arithmetic and copies ran while one was open for 14% of the time, Pallas kernels for 0%

profile of v2, /device:TPU:0, one launch (start us, length us, event | category | flops | bytes accessed | tf_op | source)
XLA Modules:
  0.0 178.5 jit_solution(18151752032644150881)
XLA Ops:
  4.0 4.6 %fusion.44 = f32[512,1024]{1,0:T(8,128)} fusion(f32[512,256]{1,0:T(8,128)} %param.4, f32[256,1024]{1,0:T(8,128)} %param.5), kind=kOutput, calls=%fused_computation.110 | convolution fusion | flops 1610612736 | bytes 3670016 | tf_op jit(solution)/shard_map/dot_general | solution.py:159
  8.8 4.9 %reshape.25.sig_hbm = f32[1024,1024]{1,0:T(8,128)} reshape(f32[1048576]{0:T(1024)} %param.3) | data formatting | bytes 8388608 | tf_op jit(solution)/shard_map/reshape | solution.py:155
  13.7 12.0 %shard_map.50 = f32[512,1024]{1,0:T(8,128)S(1)} custom-call(f32[1024,1024]{1,0:T(8,128)} %reshape.25.sig_hbm, f32[8,1024]{1,0:T(8,128)S(1)} %reshape.26.tail_ref, f32[4,1024]{1,0:T(4,128)S(1)} %multiply_subtract_fusion.win_ref, f32[32,512]{1,0:T(8,128)S(1)} %get-tuple-element.36.ca_ref, f32[32,512]{1,0:T(8,128)S(1)} %get-tuple-element.35.sa_ref, ...), custom_call_target="tpu_custom_call" | custom-call | tf_op jit(solution)/shard_map/pallas_call | solution.py:81
  25.8 3.5 %fusion.7 = f32[256,1024]{0,1:T(8,128)S(1)} fusion(f32[512,256]{1,0:T(8,128)S(1)} %copy-done, f32[512,1024]{1,0:T(8,128)S(1)} %shard_map.50, f32[512,1024]{1,0:T(8,128)S(1)} %copy-done.5), kind=kOutput, calls=%fused_computation.8 | convolution fusion | flops 1611137024 | bytes 5767168 | tf_op jit(solution)/shard_map/kr,kf->rf/dot_general | solution.py:161
  31.8 2.3 %fusion.43 = (f32[256,512]{1,0:T(8,128)}, f32[256,512]{1,0:T(8,128)}) fusion(f32[256,1024]{1,0:T(8,128)} %param.5), kind=kLoop, calls=%fused_computation.109 | loop fusion | bytes 2097152 | tf_op jit(solution)/shard_map/split | solution.py:100
  35.3 2.1 %copy.12 = f32[256,512]{0,1:T(8,128)} copy(f32[256,512]{1,0:T(8,128)} %get-tuple-element.17) | data formatting | bytes 1048576
  37.3 3.0 %collective-permute-start.4 = (f32[256]{0:T(256)S(1)}, f32[256]{0:T(256)S(1)}, u32[]{:S(2)}, u32[]{:S(2)}) collective-permute-start(f32[256]{0:T(256)S(1)} %add.142), channel_id=1, source_target_pairs={{0,16},{8,24},{16,0},{24,8},{1,17},{9,25},{17,1},{25,9},{2,18},{10... | collective-permute-start | bytes 3080 | tf_op jit(solution)/shard_map/ppermute | solution.py:114
  42.1 7.8 %collective-permute-done.2 = f32[256,256]{0,1:T(8,128)S(1)} collective-permute-done((f32[256,256]{0,1:T(8,128)S(1)}, f32[256,256]{0,1:T(8,128)S(1)}, u32[]{:S(2)}, u32[]{:S(2)}) %collective-permute-start.2) | collective-permute-done | bytes 262176 | tf_op jit(solution)/shard_map/ppermute | solution.py:114
  50.4 6.7 %collective-permute-done.5 = f32[256,256]{0,1:T(8,128)S(1)} collective-permute-done((f32[256,256]{0,1:T(8,128)S(1)}, f32[256,256]{0,1:T(8,128)S(1)}, u32[]{:S(2)}, u32[]{:S(2)}) %collective-permute-start.5) | collective-permute-done | bytes 262176 | tf_op jit(solution)/shard_map/ppermute | solution.py:139
  58.1 2.2 %collective-permute-done.6 = f32[256,512]{0,1:T(8,128)} collective-permute-done((f32[256,512]{0,1:T(8,128)}, f32[256,512]{0,1:T(8,128)}, u32[]{:S(2)}, u32[]{:S(2)}) %collective-permute-start.6) | collective-permute-done | bytes 524320 | tf_op jit(solution)/shard_map/ppermute | solution.py:139
  60.3 2.0 %broadcast_select_fusion.2 = (f32[256,512]{0,1:T(8,128)}, f32[256,512]{0,1:T(8,128)S(1)}, f32[256,512]{0,1:T(8,128)S(1)}) fusion(pred[]{:T(512)S(6)} %eq.48, f32[256,512]{0,1:T(8,128)} %collective-permute-done.6, f32[256,256]{0,1:T(8,128)} %copy-done.4, f32[256,256]{0,1:T(8,128)S(1)} %get-tuple-element.25), kind=kLoop, calls=%fused_computation.44 | loop fusion | flops 524288 | bytes 2621441 | tf_op jit(solution)/shard_map/jit(_where)/select_n | solution.py:101
  64.2 1.9 %fusion = f32[512,256]{1,0:T(8,128)S(1)} fusion(f32[512,1024]{1,0:T(8,128)S(1)} %shard_map.50, f32[1024,512]{0,1:T(8,128)S(1)} %fusion.11, f32[256,512]{0,1:T(8,128)S(1)} %get-tuple-element.14, f32[256,512]{0,1:T(8,128)S(1)} %get-tuple-element.13), kind=kOutput, calls=%fused_computation.1 | convolution fusion | flops 1611399168 | bytes 5767168 | tf_op jit(solution)/shard_map/kf,rf->kr/dot_general | solution.py:170
  66.9 2.6 %collective-permute-start.7 = (f32[256,256]{1,0:T(8,128)S(1)}, f32[256,256]{1,0:T(8,128)}, u32[]{:S(2)}, u32[]{:S(2)}) collective-permute-start(f32[256,256]{1,0:T(8,128)S(1)} %slice_select_fusion.7), channel_id=1, source_target_pairs={{0,1},{1,0},{2,3},{3,2},{4,5},{5,4},{6,7},{7,6},{8,9},{9,8},{10,11... | collective-permute-start | bytes 786440 | tf_op jit(solution)/shard_map/ppermute | solution.py:114
  70.9 5.4 %collective-permute-done.7 = f32[256,256]{1,0:T(8,128)} collective-permute-done((f32[256,256]{1,0:T(8,128)S(1)}, f32[256,256]{1,0:T(8,128)}, u32[]{:S(2)}, u32[]{:S(2)}) %collective-permute-start.7) | collective-permute-done | bytes 262176 | tf_op jit(solution)/shard_map/ppermute | solution.py:114
  78.1 2.7 %collective-permute-start.8 = (f32[128,256]{1,0:T(8,128)}, f32[128,256]{1,0:T(8,128)S(1)}, u32[]{:S(2)}, u32[]{:S(2)}) collective-permute-start(f32[128,256]{1,0:T(8,128)} %slice_select_fusion.12), channel_id=1, source_target_pairs={{0,2},{1,3},{2,0},{3,1},{4,6},{5,7},{6,4},{7,5},{8,10},{9,11},{10,... | collective-permute-start | bytes 393224 | tf_op jit(solution)/shard_map/ppermute | solution.py:114
  81.7 3.5 %collective-permute-done.11 = f32[256]{0:T(256)S(1)} collective-permute-done((f32[256]{0:T(256)S(1)}, f32[256]{0:T(256)S(1)}, u32[]{:S(2)}, u32[]{:S(2)}) %collective-permute-start.11) | collective-permute-done | bytes 1056 | tf_op jit(solution)/shard_map/ppermute | solution.py:114
  85.2 2.6 %collective-permute-start.12 = (f32[256]{0:T(256)S(1)}, f32[256]{0:T(256)S(1)}, u32[]{:S(2)}, u32[]{:S(2)}) collective-permute-start(f32[256]{0:T(256)S(1)} %add.148), channel_id=1, source_target_pairs={{0,4},{1,5},{2,6},{3,7},{4,0},{5,1},{6,2},{7,3},{8,12},{9,13},{10,... | collective-permute-start | bytes 3080 | tf_op jit(solution)/shard_map/ppermute | solution.py:114
  90.4 4.2 %collective-permute-done.9 = f32[64,256]{1,0:T(8,128)S(1)} collective-permute-done((f32[64,256]{1,0:T(8,128)S(1)}, f32[64,256]{1,0:T(8,128)S(1)}, u32[]{:S(2)}, u32[]{:S(2)}) %collective-permute-start.9) | collective-permute-done | bytes 65568 | tf_op jit(solution)/shard_map/ppermute | solution.py:114
  94.6 5.3 %collective-permute-done.13 = f32[64,256]{1,0:T(8,128)S(1)} collective-permute-done((f32[64,256]{1,0:T(8,128)S(1)}, f32[64,256]{1,0:T(8,128)S(1)}, u32[]{:S(2)}, u32[]{:S(2)}) %collective-permute-start.13) | collective-permute-done | bytes 65568 | tf_op jit(solution)/shard_map/ppermute | solution.py:139
  100.1 5.0 %collective-permute-done.14 = f32[128,256]{1,0:T(8,128)S(1)} collective-permute-done((f32[128,256]{1,0:T(8,128)S(1)}, f32[128,256]{1,0:T(8,128)S(1)}, u32[]{:S(2)}, u32[]{:S(2)}) %collective-permute-start.14) | collective-permute-done | bytes 131104 | tf_op jit(solution)/shard_map/ppermute | solution.py:139
  105.8 5.8 %collective-permute-done.15 = f32[256,256]{1,0:T(8,128)S(1)} collective-permute-done((f32[256,256]{1,0:T(8,128)S(1)}, f32[256,256]{1,0:T(8,128)S(1)}, u32[]{:S(2)}, u32[]{:S(2)}) %collective-permute-start.15) | collective-permute-done | bytes 262176 | tf_op jit(solution)/shard_map/ppermute | solution.py:139
  111.6 2.1 %fusion.10 = f32[512,1024]{1,0:T(8,128)S(1)} fusion(f32[256,512]{0,1:T(8,128)S(1)} %copy-done.2, f32[256,512]{0,1:T(8,128)S(1)} %get-tuple-element.13, f32[256,256]{1,0:T(8,128)S(1)} %get-tuple-element.9, f32[256,256]{1,0:T(8,128)S(1)} %get-tuple-element.24), kind=kOutput, calls=%fused_computation.11 | convolution fusion | flops 1611005952 | bytes 3670016 | tf_op jit(solution)/shard_map/dot_general | solution.py:159
  113.7 3.5 %fusion.3 = f32[256,1024]{0,1:T(8,128)S(1)} fusion(f32[512,1024]{1,0:T(8,128)S(1)} %shard_map.50, f32[512,1024]{1,0:T(8,128)S(1)} %fusion.10, f32[256,256]{1,0:T(8,128)S(1)} %get-tuple-element.9, f32[256,256]{1,0:T(8,128)S(1)} %get-tuple-element.24), kind=kOutput, calls=%fused_computation.4 | convolution fusion | flops 1611268096 | bytes 5767168 | tf_op jit(solution)/shard_map/kr,kf->rf/dot_general | solution.py:161
  122.7 5.2 %collective-permute-done.19 = f32[256]{0:T(256)S(1)} collective-permute-done((f32[256]{0:T(256)S(1)}, f32[256]{0:T(256)S(1)}, u32[]{:S(2)}, u32[]{:S(2)}) %collective-permute-start.19) | collective-permute-done | bytes 1056 | tf_op jit(solution)/shard_map/ppermute | solution.py:114
  128.6 6.9 %collective-permute-done.20 = f32[256,256]{0,1:T(8,128)S(1)} collective-permute-done((f32[256,256]{0,1:T(8,128)S(1)}, f32[256,256]{0,1:T(8,128)S(1)}, u32[]{:S(2)}, u32[]{:S(2)}) %collective-permute-start.20) | collective-permute-done | bytes 262176 | tf_op jit(solution)/shard_map/ppermute | solution.py:139
  143.7 6.4 %collective-permute-done.25 = f32[256]{0:T(256)S(1)} collective-permute-done((f32[256]{0:T(256)S(1)}, f32[256]{0:T(256)S(1)}, u32[]{:S(2)}, u32[]{:S(2)}) %collective-permute-start.25) | collective-permute-done | bytes 1056 | tf_op jit(solution)/shard_map/ppermute | solution.py:114
  150.1 2.1 %collective-permute-start.23 = (f32[128,256]{1,0:T(8,128)S(1)}, f32[128,256]{1,0:T(8,128)S(1)}, u32[]{:S(2)}, u32[]{:S(2)}) collective-permute-start(f32[128,256]{1,0:T(8,128)S(1)} %slice_select_fusion.11), channel_id=1, source_target_pairs={{0,2},{1,3},{2,0},{3,1},{4,6},{5,7},{6,4},{7,5},{8,10},{9,11},{10,... | collective-permute-start | bytes 393224 | tf_op jit(solution)/shard_map/ppermute | solution.py:114
  158.2 2.2 %collective-permute-done.24 = f32[64,256]{1,0:T(8,128)S(1)} collective-permute-done((f32[64,256]{1,0:T(8,128)S(1)}, f32[64,256]{1,0:T(8,128)S(1)}, u32[]{:S(2)}, u32[]{:S(2)}) %collective-permute-start.24) | collective-permute-done | bytes 65568 | tf_op jit(solution)/shard_map/ppermute | solution.py:114
  162.0 3.7 %collective-permute-done.28 = f32[64,256]{1,0:T(8,128)S(1)} collective-permute-done((f32[64,256]{1,0:T(8,128)S(1)}, f32[64,256]{1,0:T(8,128)S(1)}, u32[]{:S(2)}, u32[]{:S(2)}) %collective-permute-start.28) | collective-permute-done | bytes 65568 | tf_op jit(solution)/shard_map/ppermute | solution.py:139
  165.8 2.4 %collective-permute-start.29 = (f32[128,256]{1,0:T(8,128)S(1)}, f32[128,256]{1,0:T(8,128)S(1)}, u32[]{:S(2)}, u32[]{:S(2)}) collective-permute-start(f32[128,256]{1,0:T(8,128)S(1)} %pad_maximum_fusion.15), channel_id=1, source_target_pairs={{0,2},{1,3},{2,0},{3,1},{4,6},{5,7},{6,4},{7,5},{8,10},{9,11},{10,... | collective-permute-start | bytes 393224 | tf_op jit(solution)/shard_map/ppermute | solution.py:139
  168.2 2.9 %collective-permute-done.29 = f32[128,256]{1,0:T(8,128)S(1)} collective-permute-done((f32[128,256]{1,0:T(8,128)S(1)}, f32[128,256]{1,0:T(8,128)S(1)}, u32[]{:S(2)}, u32[]{:S(2)}) %collective-permute-start.29) | collective-permute-done | bytes 131104 | tf_op jit(solution)/shard_map/ppermute | solution.py:139
  173.3 4.4 %collective-permute-done.30 = f32[256,256]{1,0:T(8,128)S(1)} collective-permute-done((f32[256,256]{1,0:T(8,128)S(1)}, f32[256,256]{1,0:T(8,128)S(1)}, u32[]{:S(2)}, u32[]{:S(2)}) %collective-permute-start.30) | collective-permute-done | bytes 262176 | tf_op jit(solution)/shard_map/ppermute | solution.py:139
  (129 shorter events, 45.3 us)
Async XLA Ops:
  1.3 12.3 %collective-permute-start = (f32[3072]{0:T(1024)S(1)}, f32[3072]{0:T(1024)S(1)}, u32[]{:S(2)}, u32[]{:S(2)}) collective-permute-start(f32[3072]{0:T(1024)S(1)} %slice.3), channel_id=1, source_target_pairs={{1,0},{2,1},{3,2},{4,3},{5,4},{6,5},{7,6},{9,8},{10,9},{11,10},{12... | collective-permute-start | bytes 36872 | tf_op jit(solution)/shard_map/ppermute | solution.py:22
  31.1 9.2 %collective-permute-start.1 = (f32[256,512]{0,1:T(8,128)}, f32[256,512]{0,1:T(8,128)}, u32[]{:S(2)}, u32[]{:S(2)}) collective-permute-start(f32[256,512]{0,1:T(8,128)} %slice_select_fusion.1), channel_id=1, source_target_pairs={{0,8},{8,0},{16,24},{24,16},{1,9},{9,1},{17,25},{25,17},{2,10},{10... | collective-permute-start | bytes 1572872 | tf_op jit(solution)/shard_map/ppermute | solution.py:114
  31.7 5.6 %collective-permute-start.3 = (f32[256]{0:T(256)S(1)}, f32[256]{0:T(256)S(1)}, u32[]{:S(2)}, u32[]{:S(2)}) collective-permute-start(f32[256]{0:T(256)S(1)} %reduce_sum.50), channel_id=1, source_target_pairs={{0,8},{8,0},{16,24},{24,16},{1,9},{9,1},{17,25},{25,17},{2,10},{10... | collective-permute-start | bytes 3080 | tf_op jit(solution)/shard_map/ppermute | solution.py:114
  37.3 4.7 %collective-permute-start.4 = (f32[256]{0:T(256)S(1)}, f32[256]{0:T(256)S(1)}, u32[]{:S(2)}, u32[]{:S(2)}) collective-permute-start(f32[256]{0:T(256)S(1)} %add.142), channel_id=1, source_target_pairs={{0,16},{8,24},{16,0},{24,8},{1,17},{9,25},{17,1},{25,9},{2,18},{10... | collective-permute-start | bytes 3080 | tf_op jit(solution)/shard_map/ppermute | solution.py:114
  41.9 8.0 %collective-permute-start.2 = (f32[256,256]{0,1:T(8,128)S(1)}, f32[256,256]{0,1:T(8,128)S(1)}, u32[]{:S(2)}, u32[]{:S(2)}) collective-permute-start(f32[256,256]{0,1:T(8,128)S(1)} %slice_select_fusion.8), channel_id=1, source_target_pairs={{0,16},{8,24},{16,0},{24,8},{1,17},{9,25},{17,1},{25,9},{2,18},{10... | collective-permute-start | bytes 786440 | tf_op jit(solution)/shard_map/ppermute | solution.py:114
  50.0 7.2 %collective-permute-start.5 = (f32[256,256]{0,1:T(8,128)S(1)}, f32[256,256]{0,1:T(8,128)S(1)}, u32[]{:S(2)}, u32[]{:S(2)}) collective-permute-start(f32[256,256]{0,1:T(8,128)S(1)} %fusion.19), channel_id=1, source_target_pairs={{0,16},{8,24},{16,0},{24,8},{1,17},{9,25},{17,1},{25,9},{2,18},{10... | collective-permute-start | bytes 786440 | tf_op jit(solution)/shard_map/ppermute | solution.py:139
  58.1 2.3 %collective-permute-start.6 = (f32[256,512]{0,1:T(8,128)}, f32[256,512]{0,1:T(8,128)}, u32[]{:S(2)}, u32[]{:S(2)}) collective-permute-start(f32[256,512]{0,1:T(8,128)} %pad_maximum_fusion.5), channel_id=1, source_target_pairs={{0,8},{8,0},{16,24},{24,16},{1,9},{9,1},{17,25},{25,17},{2,10},{10... | collective-permute-start | bytes 1572872 | tf_op jit(solution)/shard_map/ppermute | solution.py:139
  66.9 9.4 %collective-permute-start.7 = (f32[256,256]{1,0:T(8,128)S(1)}, f32[256,256]{1,0:T(8,128)}, u32[]{:S(2)}, u32[]{:S(2)}) collective-permute-start(f32[256,256]{1,0:T(8,128)S(1)} %slice_select_fusion.7), channel_id=1, source_target_pairs={{0,1},{1,0},{2,3},{3,2},{4,5},{5,4},{6,7},{7,6},{8,9},{9,8},{10,11... | collective-permute-start | bytes 786440 | tf_op jit(solution)/shard_map/ppermute | solution.py:114
  70.8 10.8 %collective-permute-start.10 = (f32[256]{0:T(256)S(1)}, f32[256]{0:T(256)S(1)}, u32[]{:S(2)}, u32[]{:S(2)}) collective-permute-start(f32[256]{0:T(256)S(1)} %reduce_sum.63), channel_id=1, source_target_pairs={{0,1},{1,0},{2,3},{3,2},{4,5},{5,4},{6,7},{7,6},{8,9},{9,8},{10,11... | collective-permute-start | bytes 3080 | tf_op jit(solution)/shard_map/ppermute | solution.py:114
  78.1 9.7 %collective-permute-start.8 = (f32[128,256]{1,0:T(8,128)}, f32[128,256]{1,0:T(8,128)S(1)}, u32[]{:S(2)}, u32[]{:S(2)}) collective-permute-start(f32[128,256]{1,0:T(8,128)} %slice_select_fusion.12), channel_id=1, source_target_pairs={{0,2},{1,3},{2,0},{3,1},{4,6},{5,7},{6,4},{7,5},{8,10},{9,11},{10,... | collective-permute-start | bytes 393224 | tf_op jit(solution)/shard_map/ppermute | solution.py:114
  81.6 30.0 %copy-start.2 = (f32[256,512]{0,1:T(8,128)S(1)}, f32[256,512]{0,1:T(8,128)}, u32[]{:S(2)}) copy-start(f32[256,512]{0,1:T(8,128)} %copy-done.1) | copy-start | bytes 1572868
  81.6 3.6 %collective-permute-start.11 = (f32[256]{0:T(256)S(1)}, f32[256]{0:T(256)S(1)}, u32[]{:S(2)}, u32[]{:S(2)}) collective-permute-start(f32[256]{0:T(256)S(1)} %add.147), channel_id=1, source_target_pairs={{0,2},{1,3},{2,0},{3,1},{4,6},{5,7},{6,4},{7,5},{8,10},{9,11},{10,... | collective-permute-start | bytes 3080 | tf_op jit(solution)/shard_map/ppermute | solution.py:114
  85.2 5.1 %collective-permute-start.12 = (f32[256]{0:T(256)S(1)}, f32[256]{0:T(256)S(1)}, u32[]{:S(2)}, u32[]{:S(2)}) collective-permute-start(f32[256]{0:T(256)S(1)} %add.148), channel_id=1, source_target_pairs={{0,4},{1,5},{2,6},{3,7},{4,0},{5,1},{6,2},{7,3},{8,12},{9,13},{10,... | collective-permute-start | bytes 3080 | tf_op jit(solution)/shard_map/ppermute | solution.py:114
  87.9 6.7 %collective-permute-start.9 = (f32[64,256]{1,0:T(8,128)S(1)}, f32[64,256]{1,0:T(8,128)S(1)}, u32[]{:S(2)}, u32[]{:S(2)}) collective-permute-start(f32[64,256]{1,0:T(8,128)S(1)} %slice_select_fusion.16), channel_id=1, source_target_pairs={{0,4},{1,5},{2,6},{3,7},{4,0},{5,1},{6,2},{7,3},{8,12},{9,13},{10,... | collective-permute-start | bytes 196616 | tf_op jit(solution)/shard_map/ppermute | solution.py:114
  94.5 5.4 %collective-permute-start.13 = (f32[64,256]{1,0:T(8,128)S(1)}, f32[64,256]{1,0:T(8,128)S(1)}, u32[]{:S(2)}, u32[]{:S(2)}) collective-permute-start(f32[64,256]{1,0:T(8,128)S(1)} %fusion.31), channel_id=1, source_target_pairs={{0,4},{1,5},{2,6},{3,7},{4,0},{5,1},{6,2},{7,3},{8,12},{9,13},{10,... | collective-permute-start | bytes 196616 | tf_op jit(solution)/shard_map/ppermute | solution.py:139
  100.0 5.0 %collective-permute-start.14 = (f32[128,256]{1,0:T(8,128)S(1)}, f32[128,256]{1,0:T(8,128)S(1)}, u32[]{:S(2)}, u32[]{:S(2)}) collective-permute-start(f32[128,256]{1,0:T(8,128)S(1)} %pad_maximum_fusion.14), channel_id=1, source_target_pairs={{0,2},{1,3},{2,0},{3,1},{4,6},{5,7},{6,4},{7,5},{8,10},{9,11},{10,... | collective-permute-start | bytes 393224 | tf_op jit(solution)/shard_map/ppermute | solution.py:139
  105.1 6.4 %collective-permute-start.15 = (f32[256,256]{1,0:T(8,128)S(1)}, f32[256,256]{1,0:T(8,128)S(1)}, u32[]{:S(2)}, u32[]{:S(2)}) collective-permute-start(f32[256,256]{1,0:T(8,128)S(1)} %pad_maximum_fusion.12), channel_id=1, source_target_pairs={{0,1},{1,0},{2,3},{3,2},{4,5},{5,4},{6,7},{7,6},{8,9},{9,8},{10,11... | collective-permute-start | bytes 786440 | tf_op jit(solution)/shard_map/ppermute | solution.py:139
  117.3 2.0 %collective-permute-start.16 = (f32[256,512]{0,1:T(8,128)S(1)}, f32[256,512]{0,1:T(8,128)S(1)}, u32[]{:S(2)}, u32[]{:S(2)}) collective-permute-start(f32[256,512]{0,1:T(8,128)S(1)} %slice_select_fusion), channel_id=1, source_target_pairs={{0,8},{8,0},{16,24},{24,16},{1,9},{9,1},{17,25},{25,17},{2,10},{10... | collective-permute-start | bytes 1572872 | tf_op jit(solution)/shard_map/ppermute | solution.py:114
  119.4 8.5 %collective-permute-start.17 = (f32[256,256]{0,1:T(8,128)S(1)}, f32[256,256]{0,1:T(8,128)S(1)}, u32[]{:S(2)}, u32[]{:S(2)}) collective-permute-start(f32[256,256]{0,1:T(8,128)S(1)} %slice_select_fusion.6), channel_id=1, source_target_pairs={{0,16},{8,24},{16,0},{24,8},{1,17},{9,25},{17,1},{25,9},{2,18},{10... | collective-permute-start | bytes 786440 | tf_op jit(solution)/shard_map/ppermute | solution.py:114
  120.0 1.2 collective-permute-start.18
  121.2 6.7 %collective-permute-start.19 = (f32[256]{0:T(256)S(1)}, f32[256]{0:T(256)S(1)}, u32[]{:S(2)}, u32[]{:S(2)}) collective-permute-start(f32[256]{0:T(256)S(1)} %add.152), channel_id=1, source_target_pairs={{0,16},{8,24},{16,0},{24,8},{1,17},{9,25},{17,1},{25,9},{2,18},{10... | collective-permute-start | bytes 3080 | tf_op jit(solution)/shard_map/ppermute | solution.py:114
  128.0 7.5 %collective-permute-start.20 = (f32[256,256]{0,1:T(8,128)S(1)}, f32[256,256]{0,1:T(8,128)S(1)}, u32[]{:S(2)}, u32[]{:S(2)}) collective-permute-start(f32[256,256]{0,1:T(8,128)S(1)} %fusion.17), channel_id=1, source_target_pairs={{0,16},{8,24},{16,0},{24,8},{1,17},{9,25},{17,1},{25,9},{2,18},{10... | collective-permute-start | bytes 786440 | tf_op jit(solution)/shard_map/ppermute | solution.py:139
  135.6 2.0 %collective-permute-start.21 = (f32[256,512]{0,1:T(8,128)S(1)}, f32[256,512]{0,1:T(8,128)S(1)}, u32[]{:S(2)}, u32[]{:S(2)}) collective-permute-start(f32[256,512]{0,1:T(8,128)S(1)} %pad_maximum_fusion.7), channel_id=1, source_target_pairs={{0,8},{8,0},{16,24},{24,16},{1,9},{9,1},{17,25},{25,17},{2,10},{10... | collective-permute-start | bytes 1572872 | tf_op jit(solution)/shard_map/ppermute | solution.py:139
  141.6 8.5 %collective-permute-start.22 = (f32[256,256]{1,0:T(8,128)S(1)}, f32[256,256]{1,0:T(8,128)S(1)}, u32[]{:S(2)}, u32[]{:S(2)}) collective-permute-start(f32[256,256]{1,0:T(8,128)S(1)} %slice_select_fusion.5), channel_id=1, source_target_pairs={{0,1},{1,0},{2,3},{3,2},{4,5},{5,4},{6,7},{7,6},{8,9},{9,8},{10,11... | collective-permute-start | bytes 786440 | tf_op jit(solution)/shard_map/ppermute | solution.py:114
  142.3 7.8 %collective-permute-start.25 = (f32[256]{0:T(256)S(1)}, f32[256]{0:T(256)S(1)}, u32[]{:S(2)}, u32[]{:S(2)}) collective-permute-start(f32[256]{0:T(256)S(1)} %reduce_sum.69), channel_id=1, source_target_pairs={{0,1},{1,0},{2,3},{3,2},{4,5},{5,4},{6,7},{7,6},{8,9},{9,8},{10,11... | collective-permute-start | bytes 3080 | tf_op jit(solution)/shard_map/ppermute | solution.py:114
  150.1 3.6 %collective-permute-start.26 = (f32[256]{0:T(256)S(1)}, f32[256]{0:T(256)S(1)}, u32[]{:S(2)}, u32[]{:S(2)}) collective-permute-start(f32[256]{0:T(256)S(1)} %add.157), channel_id=1, source_target_pairs={{0,2},{1,3},{2,0},{3,1},{4,6},{5,7},{6,4},{7,5},{8,10},{9,11},{10,... | collective-permute-start | bytes 3080 | tf_op jit(solution)/shard_map/ppermute | solution.py:114
  150.1 5.0 %collective-permute-start.23 = (f32[128,256]{1,0:T(8,128)S(1)}, f32[128,256]{1,0:T(8,128)S(1)}, u32[]{:S(2)}, u32[]{:S(2)}) collective-permute-start(f32[128,256]{1,0:T(8,128)S(1)} %slice_select_fusion.11), channel_id=1, source_target_pairs={{0,2},{1,3},{2,0},{3,1},{4,6},{5,7},{6,4},{7,5},{8,10},{9,11},{10,... | collective-permute-start | bytes 393224 | tf_op jit(solution)/shard_map/ppermute | solution.py:114
  153.6 4.6 %collective-permute-start.27 = (f32[256]{0:T(256)S(1)}, f32[256]{0:T(256)S(1)}, u32[]{:S(2)}, u32[]{:S(2)}) collective-permute-start(f32[256]{0:T(256)S(1)} %add.158), channel_id=1, source_target_pairs={{0,4},{1,5},{2,6},{3,7},{4,0},{5,1},{6,2},{7,3},{8,12},{9,13},{10,... | collective-permute-start | bytes 3080 | tf_op jit(solution)/shard_map/ppermute | solution.py:114
  155.2 5.2 %collective-permute-start.24 = (f32[64,256]{1,0:T(8,128)S(1)}, f32[64,256]{1,0:T(8,128)S(1)}, u32[]{:S(2)}, u32[]{:S(2)}) collective-permute-start(f32[64,256]{1,0:T(8,128)S(1)} %slice_select_fusion.15), channel_id=1, source_target_pairs={{0,4},{1,5},{2,6},{3,7},{4,0},{5,1},{6,2},{7,3},{8,12},{9,13},{10,... | collective-permute-start | bytes 196616 | tf_op jit(solution)/shard_map/ppermute | solution.py:114
  160.5 5.2 %collective-permute-start.28 = (f32[64,256]{1,0:T(8,128)S(1)}, f32[64,256]{1,0:T(8,128)S(1)}, u32[]{:S(2)}, u32[]{:S(2)}) collective-permute-start(f32[64,256]{1,0:T(8,128)S(1)} %fusion.29), channel_id=1, source_target_pairs={{0,4},{1,5},{2,6},{3,7},{4,0},{5,1},{6,2},{7,3},{8,12},{9,13},{10,... | collective-permute-start | bytes 196616 | tf_op jit(solution)/shard_map/ppermute | solution.py:139
  165.8 5.4 %collective-permute-start.29 = (f32[128,256]{1,0:T(8,128)S(1)}, f32[128,256]{1,0:T(8,128)S(1)}, u32[]{:S(2)}, u32[]{:S(2)}) collective-permute-start(f32[128,256]{1,0:T(8,128)S(1)} %pad_maximum_fusion.15), channel_id=1, source_target_pairs={{0,2},{1,3},{2,0},{3,1},{4,6},{5,7},{6,4},{7,5},{8,10},{9,11},{10,... | collective-permute-start | bytes 393224 | tf_op jit(solution)/shard_map/ppermute | solution.py:139
  171.2 6.4 %collective-permute-start.30 = (f32[256,256]{1,0:T(8,128)S(1)}, f32[256,256]{1,0:T(8,128)S(1)}, u32[]{:S(2)}, u32[]{:S(2)}) collective-permute-start(f32[256,256]{1,0:T(8,128)S(1)} %pad_maximum_fusion.13), channel_id=1, source_target_pairs={{0,1},{1,0},{2,3},{3,2},{4,5},{5,4},{6,7},{7,6},{8,9},{9,8},{10,11... | collective-permute-start | bytes 786440 | tf_op jit(solution)/shard_map/ppermute | solution.py:139
  (8 other events, 46.0 us)
